TPU v7x, 512 devices: a whole 4x4x16 slice. The times are simulated.
512 devices in a mesh: row: 32 (over z_lo, x), col: 16 (over y, z_hi, core).
Axes of the slice: x: 4, y: 4, z: 16 (z_hi: 2, z_lo: 8; z = z_hi * 8 + z_lo), core: 2. Of those that a mesh axis runs over, the one named last changes fastest.
Arguments:
- anc_inv: bfloat16 [16384, 16384], P('row', 'col'), may hold values from -0.0546875 to 0.0546875
- panel: bfloat16 [1, 12288, 2048], P(None, 'col', 'row'), may hold values from -6 to 6
- structure: int32 [1, 96], replicated, may hold values from 0 to 127, as said below
Outputs:
- off_inv: float32 [1, 16384, 2048], P(None, 'row', 'col')
Inputs may be any that keep to these rules, and one draw needn't show every extreme that they name: Each structure[s] holds 96 distinct ancestor block indices, in the order in which the panel stores its row blocks (not sorted); each group of 8 consecutive ancestor blocks holds 5 to 7 of them, and some group of each supernode holds exactly 7.
All inputs are finite; a program needn't handle non-finite values.
Results may differ from a plain program's by a relative error of at most 0.0003.
Values may be sent and summed in bfloat16 or wider, within the bound.
No kernel may reach another device: no remote copies, remote signals or barrier semaphores. Data moves between devices by JAX's collectives and lax.ppermute only.
A program may use at most 64 MiB of HBM per device.

v0:
```python
import jax
import jax.numpy as jnp
from jax import lax
from jax.sharding import Mesh, PartitionSpec as P

BS = 128
SBLK = 96
ROW = ("zl", "x")
COL = ("y", "zh", "c")


def body(anc_inv, panel, structure):
    col_index = lax.axis_index(COL)
    row_index = lax.axis_index(ROW)
    local_rows, local_cols = anc_inv.shape
    group_blocks = local_cols // BS
    local_width = panel.shape[2]
    gathered = lax.all_gather(panel, COL, axis=1, tiled=True)
    own_blocks = row_index * (local_rows // BS) + jnp.arange(local_rows // BS, dtype=jnp.int32)
    block_ids = jnp.arange(group_blocks, dtype=jnp.int32)
    blocks_of = structure[0]
    compact = gathered[0].reshape(SBLK, BS * local_width)
    local_block = blocks_of - col_index * group_blocks
    picker = (local_block[None, :] == block_ids[:, None]).astype(jnp.bfloat16)
    picked = (
        jnp.dot(picker, compact, preferred_element_type=jnp.float32)
        .astype(jnp.bfloat16)
        .reshape(group_blocks * BS, local_width)
    )
    partial_value = jnp.dot(
        anc_inv,
        lax.all_gather(lax.all_gather(picked, "x", axis=1, tiled=True), "zl", axis=1, tiled=True),
        preferred_element_type=jnp.float32,
    )
    summed = lax.psum_scatter(partial_value, COL, scatter_dimension=1, tiled=True)
    member = jnp.any(blocks_of[None, :] == own_blocks[:, None], axis=1)
    row_mask = jnp.repeat(member, BS)
    results = [jnp.where(row_mask[:, None], -summed, jnp.zeros_like(summed))]
    return jnp.stack(results)


def solution(mesh):
    rows, cols = (mesh.shape["row"], mesh.shape["col"])
    fine = Mesh(mesh.devices.reshape(rows // 4, 4, cols // 4, 2, 2), ("zl", "x", "y", "zh", "c"))
    in_specs = (P(ROW, COL), P(None, COL, ROW), P())
    out_specs = P(None, ROW, COL)
    return jax.shard_map(body, mesh=fine, in_specs=in_specs, out_specs=out_specs, check_vma=False)
```

profile of v0, /device:TPU:2, one launch (start us, length us, event | category | flops | bytes accessed | tf_op | source)
XLA Modules:
  0.0 381.6 jit_solution(18023949575931893657)
XLA Ops:
  6.5 0.0 copy-start
  6.5 0.0 all-gather.3.cloned.1.call-start
  6.5 0.7 all-gather.3.cloned.1.call-update
  7.3 0.0 all-gather.5.cloned.1.call-start
  7.3 0.7 subtract_bitcast_fusion
  8.0 92.1 %all-gather.3.cloned.1.call-done = bf16[1,12288,64]{1,2,0:T(8,128)(2,1)} async-done(((bf16[1,768,64]{1,2,0:T(8,128)(2,1)}), bf16[1,12288,64]{1,2,0:T(8,128)(2,1)}) %all-gather.3.cloned.1.call-update) | async-done | bytes 1572880 | tf_op jit(solution)/shard_map/all_gather | solution.py:18
  100.1 4.1 %copy.10 = bf16[1,12288,64]{2,1,0:T(8,128)(2,1)} copy(bf16[1,12288,64]{1,2,0:T(8,128)(2,1)} %all-gather.3.cloned.1.call-done) | data formatting | bytes 3145728 | tf_op jit(solution)/shard_map/all_gather | solution.py:18
  104.2 4.3 %reshape_squeeze.3 = bf16[96,8192]{1,0:T(8,128)(2,1)S(1)} reshape(bf16[1,12288,64]{2,1,0:T(8,128)(2,1)} %copy.10) | data formatting | bytes 3145728 | tf_op jit(solution)/shard_map/reshape;squeeze | solution.py:22
  108.4 0.3 convolution_convert_fusion
  108.7 0.3 reshape.8
  109.0 0.1 copy.11
  109.1 13.8 %all_gather.10 = bf16[1024,256]{0,1:T(8,128)(2,1)} all-gather(bf16[1024,64]{0,1:T(8,128)(2,1)S(1)} %copy.11), channel_id=1, replica_groups=mesh['zl'=8,'x'=4,'y'=4,'zh'=2,'c'=2] {'x'}, dimensions={1}, use_global_device_ids=true | all-gather | bytes 655360 | tf_op jit(solution)/shard_map/all_gather | solution.py:32
  123.0 0.0 all-gather.5.cloned.1.call-update
  123.0 0.0 reduce-scatter.2.cloned.1.call-start
  123.0 95.2 %all-gather.5.cloned.1.call-done = bf16[1024,2048]{0,1:T(8,128)(2,1)} async-done(((bf16[1024,256]{0,1:T(8,128)(2,1)}), bf16[1024,2048]{0,1:T(8,128)(2,1)}) %all-gather.5.cloned.1.call-update) | async-done | bytes 4194320 | tf_op jit(solution)/shard_map/all_gather | solution.py:32
  218.2 0.0 copy-done
  218.2 6.5 %convolution_bitcast_fusion = f32[512,2048]{0,1:T(8,128)} fusion(bf16[1024,2048]{0,1:T(8,128)(2,1)} %all-gather.5.cloned.1.call-done, bf16[512,1024]{1,0:T(8,128)(2,1)S(1)} %copy-done), kind=kOutput, calls=%fused_computation.1 | convolution fusion | flops 2147483648 | bytes 9437184 | tf_op jit(solution)/shard_map/dot_general | solution.py:30
  224.8 0.0 copy-start.1
  224.8 0.0 reduce-scatter.2.cloned.1.call-update
  224.8 0.6 copy-done.1
  225.4 0.2 compare_reduce_fusion
  225.6 0.1 broadcast_bitcast_fusion
  225.7 147.5 %reduce-scatter.2.cloned.1.call-done = f32[512,128]{0,1:T(8,128)} async-done(((f32[512,2048]{0,1:T(8,128)}), f32[512,128]{0,1:T(8,128)}) %reduce-scatter.2.cloned.1.call-update) | async-done | bytes 262160 | tf_op jit(solution)/shard_map/reduce_scatter | solution.py:35
  373.2 1.0 select_bitcast_fusion
  374.2 0.8 copy.12
  (1 shorter events, 0.0 us)
Async XLA Ops:
  6.5 211.7 %copy-start = (bf16[512,1024]{1,0:T(8,128)(2,1)S(1)}, bf16[512,1024]{1,0:T(8,128)(2,1)}, u32[]{:S(2)}) copy-start(bf16[512,1024]{1,0:T(8,128)(2,1)} %param.3) | copy-start | bytes 3145732
  6.5 93.5 %all-gather.3.cloned.1.call-start = ((), (), s32[]{:S(2)}) async-start(), calls=%async_computation.1 | async-start | bytes 1671168 | tf_op jit(solution)/shard_map/all_gather | solution.py:18
  7.3 210.9 %all-gather.5.cloned.1.call-start = ((), (), s32[]{:S(2)}) async-start(), calls=%async_computation.2 | async-start | bytes 4718592 | tf_op jit(solution)/shard_map/all_gather | solution.py:32
  123.0 250.2 %reduce-scatter.2.cloned.1.call-start = ((), (), s32[]{:S(2)}) async-start(), calls=%async_computation.3 | async-start | bytes 4456448 | tf_op jit(solution)/shard_map/reduce_scatter | solution.py:35
  224.8 0.7 copy-start.1
Sparse Core Ops, SparseCore 0:
  10.6 89.3 all-gather.2
  123.1 95.0 all-gather.4
  224.9 148.2 reduce-scatter.1
where the time goes:
time: 382 us
  waiting for transfers between devices  336 us (88%)
  blocking collectives  13.8 us (4%)
  between operations  13.2 us (3%)
  local copies, waits for them, and re-layouts  10.3 us (3%)
  matrix products  6.86 us (2%)
    reduce_scatter x1, waiting for transfers between devices, body(): lax.psum_scatter(partial_value, COL, scatter_dimension=1, tiled=True)  148 us
    all_gather x1, waiting for transfers between devices, body(): lax.all_gather(lax.all_gather(picked, 'x', axis=1, tiled=True), 'zl', axi...  95.2 us
    all_gather x1, waiting for transfers between devices, body(): gathered = lax.all_gather(panel, COL, axis=1, tiled=True)  92.1 us
    all_gather x1, blocking collectives, body(): lax.all_gather(picked, 'x', axis=1, tiled=True)  13.8 us
  transfers between devices with their start and end apart: 3, of which 3 were waited for; matrix products, arithmetic and copies ran while one was open for 0% of the time, Pallas kernels for 0%

commit v1 on v0

--- a/solution.py
+++ b/solution.py
@@ -15,7 +15,16 @@
     local_rows, local_cols = anc_inv.shape
     group_blocks = local_cols // BS
     local_width = panel.shape[2]
-    gathered = lax.all_gather(panel, COL, axis=1, tiled=True)
+
+    def feed_squares_on(xs):
+        return jnp.concatenate(
+            lax.all_to_all(
+                jnp.stack([xs] * lax.axis_size(COL), 0), COL, concat_axis=0, split_axis=0
+            ),
+            1,
+        )
+
+    gathered = feed_squares_on(panel)
     own_blocks = row_index * (local_rows // BS) + jnp.arange(local_rows // BS, dtype=jnp.int32)
     block_ids = jnp.arange(group_blocks, dtype=jnp.int32)
     blocks_of = structure[0]

time: 382 us -> 390 us (1.021)
  starting transfers between devices: 0.08 us -> 17.9 us
  waiting for transfers between devices: 336 us -> 325 us
    all_gather x1 -> x0, waiting for transfers between devices: 92.1 us -> none  [body(): gathered = lax.all_gather(panel, COL, axis=1, tiled=True)]
    all_gather x1, waiting for transfers between devices: 95.2 us -> 137 us  [body(): lax.all_gather(lax.all_gather(picked, 'x', axis=1, tiled=True), 'zl', axi...]
    all_to_all x0 -> x1, waiting for transfers between devices: none -> 40.8 us  [feed_squares_on(): lax.all_to_all(jnp.stack([xs] * lax.axis_size(COL), 0), COL, concat_axis=...]
    all_to_all x0 -> x1, starting transfers between devices: none -> 17.8 us  [feed_squares_on(): lax.all_to_all(jnp.stack([xs] * lax.axis_size(COL), 0), COL, concat_axis=...]
    all_gather x1 -> x0, local copies, waits for them, and re-layouts: 4.12 us -> none  [body(): gathered = lax.all_gather(panel, COL, axis=1, tiled=True)]
where the time goes in v1:
time: 390 us
  waiting for transfers between devices  325 us (83%)
  starting transfers between devices  17.9 us (5%)
  blocking collectives  14.3 us (4%)
  between operations  13.5 us (3%)
  local copies, waits for them, and re-layouts  10.7 us (3%)
  matrix products  6.84 us (2%)
    reduce_scatter x1, waiting for transfers between devices, body(): lax.psum_scatter(partial_value, COL, scatter_dimension=1, tiled=True)  148 us
    all_gather x1, waiting for transfers between devices, body(): lax.all_gather(lax.all_gather(picked, 'x', axis=1, tiled=True), 'zl', axi...  137 us
    all_to_all x1, waiting for transfers between devices, feed_squares_on(): lax.all_to_all(jnp.stack([xs] * lax.axis_size(COL), 0), COL, concat_axis=...  40.8 us
    all_to_all x1, starting transfers between devices, feed_squares_on(): lax.all_to_all(jnp.stack([xs] * lax.axis_size(COL), 0), COL, concat_axis=...  17.8 us
    all_gather x1, blocking collectives, body(): lax.all_gather(picked, 'x', axis=1, tiled=True)  14.3 us
  transfers between devices with their start and end apart: 3, of which 3 were waited for; matrix products, arithmetic and copies ran while one was open for 0% of the time, Pallas kernels for 0%

profile of v1, /device:TPU:2, one launch (start us, length us, event | category | flops | bytes accessed | tf_op | source)
XLA Modules:
  0.0 389.7 jit_solution(8852910109037708757)
XLA Ops:
  6.5 0.0 copy-start
  6.5 0.0 copy-start.1
  6.5 2.3 stack.4
  8.9 17.8 %all-to-all-start = ((bf16[16,1,768,64]{2,3,1,0:T(8,128)(2,1)}), bf16[16,1,768,64]{2,3,1,0:T(8,128)(2,1)S(1)}, u32[]{:S(2)}, u32[]{:S(2)}) async-start(bf16[16,1,768,64]{2,3,1,0:T(8,128)(2,1)} %stack.4), calls=%async_computation | async-start | bytes 3145728 | tf_op jit(solution)/shard_map/all_to_all | solution.py:21
  26.7 0.0 all-gather.2.cloned.1.call-start
  26.7 0.0 copy-done.1
  26.8 40.8 %all-to-all-done = bf16[16,1,768,64]{2,3,1,0:T(8,128)(2,1)S(1)} async-done(((bf16[16,1,768,64]{2,3,1,0:T(8,128)(2,1)}), bf16[16,1,768,64]{2,3,1,0:T(8,128)(2,1)S(1)}, u32[]{:S(2)}, u32[]{:S(2)}) %all-to-all-start) | async-done | bytes 1572896 | tf_op jit(solution)/shard_map/all_to_all | solution.py:21
  67.5 2.8 copy.11
  70.4 4.3 %reshape_squeeze_reshape.3 = bf16[96,8192]{1,0:T(8,128)(2,1)S(1)} reshape(bf16[16,1,768,64]{3,2,0,1:T(8,128)(2,1)} %copy.11) | data formatting | bytes 3145728 | tf_op jit(solution)/shard_map/reshape;squeeze;reshape | solution.py:31
  74.6 0.3 convolution_convert_fusion
  74.9 0.3 reshape.11
  75.2 0.1 copy.12
  75.3 14.3 %all_gather.6 = bf16[1024,256]{0,1:T(8,128)(2,1)} all-gather(bf16[1024,64]{0,1:T(8,128)(2,1)S(1)} %copy.12), channel_id=1, replica_groups=mesh['zl'=8,'x'=4,'y'=4,'zh'=2,'c'=2] {'x'}, dimensions={1}, use_global_device_ids=true | all-gather | bytes 655360 | tf_op jit(solution)/shard_map/all_gather | solution.py:41
  89.6 0.0 all-gather.2.cloned.1.call-update
  89.6 0.0 reduce-scatter.2.cloned.1.call-start
  89.7 136.7 %all-gather.2.cloned.1.call-done = bf16[1024,2048]{0,1:T(8,128)(2,1)} async-done(((bf16[1024,256]{0,1:T(8,128)(2,1)}), bf16[1024,2048]{0,1:T(8,128)(2,1)}) %all-gather.2.cloned.1.call-update) | async-done | bytes 4194320 | tf_op jit(solution)/shard_map/all_gather | solution.py:41
  226.4 0.0 copy-done
  226.4 6.5 %convolution_bitcast_fusion = f32[512,2048]{0,1:T(8,128)} fusion(bf16[1024,2048]{0,1:T(8,128)(2,1)} %all-gather.2.cloned.1.call-done, bf16[512,1024]{1,0:T(8,128)(2,1)S(1)} %copy-done), kind=kOutput, calls=%fused_computation.1 | convolution fusion | flops 2147483648 | bytes 9437184 | tf_op jit(solution)/shard_map/dot_general | solution.py:39
  232.9 0.0 reduce-scatter.2.cloned.1.call-update
  232.9 0.2 compare_reduce_fusion
  233.1 0.1 broadcast_bitcast_fusion
  233.2 147.8 %reduce-scatter.2.cloned.1.call-done = f32[512,128]{0,1:T(8,128)} async-done(((f32[512,2048]{0,1:T(8,128)}), f32[512,128]{0,1:T(8,128)}) %reduce-scatter.2.cloned.1.call-update) | async-done | bytes 262160 | tf_op jit(solution)/shard_map/reduce_scatter | solution.py:44
  381.0 1.0 select_bitcast_fusion
  382.0 0.8 copy.13
  (2 shorter events, 0.0 us)
Async XLA Ops:
  6.5 219.8 %copy-start = (bf16[512,1024]{1,0:T(8,128)(2,1)S(1)}, bf16[512,1024]{1,0:T(8,128)(2,1)}, u32[]{:S(2)}) copy-start(bf16[512,1024]{1,0:T(8,128)(2,1)} %param.3) | copy-start | bytes 3145732
  6.5 20.2 %copy-start.1 = (s32[1,96]{1,0:T(1,128)S(1)}, s32[1,96]{1,0:T(1,128)}, u32[]{:S(2)}) copy-start(s32[1,96]{1,0:T(1,128)} %param.5) | copy-start | bytes 1156
  8.9 58.7 %all-to-all-start = ((bf16[16,1,768,64]{2,3,1,0:T(8,128)(2,1)}), bf16[16,1,768,64]{2,3,1,0:T(8,128)(2,1)S(1)}, u32[]{:S(2)}, u32[]{:S(2)}) async-start(bf16[16,1,768,64]{2,3,1,0:T(8,128)(2,1)} %stack.4), calls=%async_computation | async-start | bytes 3145728 | tf_op jit(solution)/shard_map/all_to_all | solution.py:21
  26.7 199.7 %all-gather.2.cloned.1.call-start = ((), (), s32[]{:S(2)}) async-start(), calls=%async_computation.2 | async-start | bytes 4718592 | tf_op jit(solution)/shard_map/all_gather | solution.py:41
  89.6 291.4 %reduce-scatter.2.cloned.1.call-start = ((), (), s32[]{:S(2)}) async-start(), calls=%async_computation.3 | async-start | bytes 4456448 | tf_op jit(solution)/shard_map/reduce_scatter | solution.py:44
Sparse Core Ops, SparseCore 0:
  89.7 136.5 all-gather.1
  233.0 147.9 reduce-scatter.1
